TPU v7x, 32 devices: a whole 2x2x4 slice. The times are simulated.
32 devices in a mesh: section: 4 (over y, core), seq: 8 (over z, x).
Axes of the slice: x: 2, y: 2, z: 4, core: 2. Of those that a mesh axis runs over, the one named last changes fastest.
Arguments:
- queries: bfloat16 [4, 2048, 4096], P('section', 'seq'), may hold values from -42 to 42
- keys: bfloat16 [4, 2048, 512], P('section', 'seq'), may hold values from -6 to 6
- values: bfloat16 [4, 2048, 512], P('section', 'seq'), may hold values from -6 to 6
- out_grads: bfloat16 [4, 2048, 4096], P('section', 'seq'), may hold values from -6 to 6
- random_blocks: int32 [4, 32, 3], P('section'), may hold values from 0 to 31, as said below
- global_blocks: int32 [4, 2], P('section'), may hold values from 0 to 31, as said below
- pad_lengths: int32 [4, 8], P('section'), may hold values from 0 to 63, as said below
Outputs:
- passed_query_grad: bfloat16 [4, 2048, 4096], P('section', 'seq')
- passed_key_grad: bfloat16 [4, 2048, 512], P('section', 'seq')
- passed_value_grad: bfloat16 [4, 2048, 512], P('section', 'seq')
Inputs may be any that keep to these rules, and one draw needn't show every extreme that they name: `random_blocks`: over the 12 random blocks named by one shard's query blocks, the blocks of any one shard are named at most 2 times, and on every shard some shard's blocks exactly 2 times; within one random slot (one column) at most 1 times, and exactly 1 times for some shard. `global_blocks`: the 2 global blocks of a section are distinct. `pad_lengths`: every section has a shard with exactly 63 padding tokens.
All inputs are finite; a program needn't handle non-finite values.
Results may differ from a plain program's by a relative error of at most 0.007.
Values may be sent and summed in bfloat16 or wider, within the bound.
No kernel may reach another device: no remote copies, remote signals or barrier semaphores. Data moves between devices by JAX's collectives and lax.ppermute only.
A program may use at most 128 MiB of HBM per device.

v0:
```python
import math
import jax
import jax.numpy as jnp
from jax import lax
from jax.sharding import PartitionSpec as P

HDIM = 128
BLK = 64
GLOB = 2
RAND = 3


def extended_2(array, sides, width):
    for axis, dim in sides:
        devices, length = (lax.axis_size(axis), array.shape[dim])
        up = [(i, (i + 1) % devices) for i in range(devices - 1)]
        down = [(j, i) for i, j in up]
        last = lax.slice_in_dim(array, length - width, length, axis=dim)
        leading = lax.slice_in_dim(array, 0, width, axis=dim)
        before = lax.ppermute(last, axis, up)
        after = lax.ppermute(leading, axis, down)
        array = jnp.concatenate([before, array, after], axis=dim)
    return array


def broadcast(array, axis, root):
    mine = lax.axis_index(axis) == root
    return lax.psum(jnp.where(mine, array, jnp.zeros_like(array)), axis)


def from_behind(block, axis, distance):
    devices = range(lax.axis_size(axis))
    route = [((i - distance) % len(devices), i) for i in devices]
    return lax.ppermute(block, axis, route)


def block_backward(query_rows, grad_rows, key_tiles, value_tiles, key_live):
    nblocks, block_len, qwidth = query_rows.shape
    ntiles = key_tiles.shape[1]
    kwidth = key_tiles.shape[-1]
    heads_kv = kwidth // HDIM
    group = qwidth // kwidth
    score_scale = 1.0 / math.sqrt(HDIM)
    query_heads = jnp.moveaxis(query_rows.reshape(nblocks, block_len, heads_kv, group, HDIM), 2, 0)
    grad_heads = jnp.moveaxis(grad_rows.reshape(nblocks, block_len, heads_kv, group, HDIM), 2, 0)
    key_heads = jnp.moveaxis(key_tiles.reshape(nblocks, ntiles, block_len, heads_kv, HDIM), 3, 0)
    value_heads = jnp.moveaxis(
        value_tiles.reshape(nblocks, ntiles, block_len, heads_kv, HDIM), 3, 0
    )
    live_mask = key_live[:, None, None, :, :]

    def one_head(inputs):
        query_one, grad_one, key_one, value_one = inputs
        scores = (
            jnp.einsum("bqgd,btkd->bgqtk", query_one, key_one, preferred_element_type=jnp.float32)
            * score_scale
        )
        scores = jnp.where(live_mask, scores, -1e30)
        row_max = jnp.max(scores, axis=(3, 4), keepdims=True)
        log_total = row_max + jnp.log(
            jnp.sum(jnp.exp(scores - row_max), axis=(3, 4), keepdims=True)
        )
        probs = jnp.exp(scores - log_total)
        probs_low = probs.astype(jnp.bfloat16)
        output = jnp.einsum(
            "bgqtk,btkd->bqgd", probs_low, value_one, preferred_element_type=jnp.float32
        )
        row_dot = jnp.sum(grad_one * output, axis=-1)
        prob_grad = jnp.einsum(
            "bqgd,btkd->bgqtk", grad_one, value_one, preferred_element_type=jnp.float32
        )
        score_grad = (
            probs * (prob_grad - jnp.transpose(row_dot, (0, 2, 1))[:, :, :, None, None])
        ).astype(jnp.bfloat16)
        query_grad = (
            jnp.einsum("bgqtk,btkd->bqgd", score_grad, key_one, preferred_element_type=jnp.float32)
            * score_scale
        )
        key_grad = (
            jnp.einsum(
                "bgqtk,bqgd->btkd", score_grad, query_one, preferred_element_type=jnp.float32
            )
            * score_scale
        )
        value_grad = jnp.einsum(
            "bgqtk,bqgd->btkd", probs_low, grad_one, preferred_element_type=jnp.float32
        )
        return (query_grad, key_grad, value_grad)

    query_grad, key_grad, value_grad = lax.map(
        one_head, (query_heads, grad_heads, key_heads, value_heads)
    )
    return (
        jnp.moveaxis(query_grad, 0, 2).reshape(nblocks, block_len, qwidth),
        jnp.moveaxis(key_grad, 0, 3).reshape(nblocks, ntiles, block_len, kwidth),
        jnp.moveaxis(value_grad, 0, 3).reshape(nblocks, ntiles, block_len, kwidth),
    )


def request_plan(request_lists, this_shard, query_blocks):
    shards, count = request_lists.shape
    capacity = -(-count // shards)
    owner_ids = request_lists // query_blocks
    local_ids = request_lists % query_blocks
    order = jnp.arange(count, dtype=jnp.int32)
    earlier = order[None, :] < order[:, None]
    same_owner = owner_ids[:, :, None] == owner_ids[:, None, :]
    slot_rank = jnp.sum(same_owner & earlier[None], axis=2)
    slot_ids = jnp.arange(capacity, dtype=jnp.int32)
    chosen = (owner_ids[:, None, :] == this_shard) & (
        slot_rank[:, None, :] == slot_ids[None, :, None]
    )
    serve_block = jnp.sum(jnp.where(chosen, local_ids[:, None, :], 0), axis=2)
    slot_used = jnp.any(chosen, axis=2)
    owner_mine = lax.dynamic_index_in_dim(owner_ids, this_shard, 0, keepdims=False)
    rank_mine = lax.dynamic_index_in_dim(slot_rank, this_shard, 0, keepdims=False)
    return (serve_block, slot_used, owner_mine, rank_mine)


def serve_tiles(own_blocks, request_info):
    serve_block, slot_used = (request_info[0], request_info[1])
    shards, capacity = serve_block.shape
    gathered = jnp.take(own_blocks, serve_block.reshape(-1), axis=1)
    gathered = gathered.reshape(2, shards, capacity, own_blocks.shape[2], own_blocks.shape[3])
    return jnp.where(slot_used[None, :, :, None, None], gathered, jnp.zeros((), own_blocks.dtype))


def pick_tiles(received, request_info):
    return received[:, request_info[2], request_info[3]]


def place_terms(terms, request_info):
    serve_block = request_info[0]
    shards, capacity = serve_block.shape
    holder = jnp.zeros((2, shards, capacity, terms.shape[2], terms.shape[3]), terms.dtype)
    return holder.at[:, request_info[2], request_info[3]].set(terms)


def absorb_terms(received, request_info, query_blocks):
    serve_block, slot_used = (request_info[0], request_info[1])
    onehot = (
        slot_used[:, :, None]
        & (serve_block[:, :, None] == jnp.arange(query_blocks, dtype=jnp.int32)[None, None, :])
    ).astype(jnp.bfloat16)
    return jnp.einsum("ncq,xncsk->xqsk", onehot, received, preferred_element_type=jnp.float32)


def token_live(tile_ids, pad_sizes, query_blocks, shard_tokens, total_blocks):
    valid = (tile_ids >= 0) & (tile_ids < total_blocks)
    safe_ids = jnp.clip(tile_ids, 0, total_blocks - 1)
    owner_shard = safe_ids // query_blocks
    shards = pad_sizes.shape[0]
    pad_of = jnp.sum(
        jnp.where(owner_shard[..., None] == jnp.arange(shards, dtype=jnp.int32), pad_sizes, 0),
        axis=-1,
    )
    within = (safe_ids % query_blocks)[..., None] * BLK + jnp.arange(BLK, dtype=jnp.int32)
    return valid[..., None] & (within < (shard_tokens - pad_of)[..., None])


def body(queries, keys, values, out_grads, random_blocks, global_blocks, pad_lengths):
    query_rows = queries[0]
    key_rows = keys[0]
    value_rows = values[0]
    grad_rows = out_grads[0]
    random_table = random_blocks[0]
    global_ids = global_blocks[0]
    pad_sizes = pad_lengths[0]
    shards = lax.axis_size("seq")
    this_shard = lax.axis_index("seq")
    shard_tokens, qwidth = query_rows.shape
    kwidth = key_rows.shape[1]
    query_blocks = shard_tokens // BLK
    total_blocks = query_blocks * shards
    near = 3 + GLOB
    kvpair = jnp.stack([key_rows, value_rows])
    extended = extended_2(kvpair, (("seq", 1),), BLK)
    ext_blocks = extended.reshape(2, query_blocks + 2, BLK, kwidth)
    window = jnp.stack(
        [ext_blocks[:, offset : offset + query_blocks] for offset in range(3)], axis=2
    )
    own_blocks = kvpair.reshape(2, query_blocks, BLK, kwidth)
    global_list = []
    for glob_num in range(GLOB):
        owner_dev = global_ids[glob_num] // query_blocks
        local_tile = lax.dynamic_index_in_dim(
            own_blocks, global_ids[glob_num] % query_blocks, 1, keepdims=False
        )
        global_list.append(broadcast(local_tile, "seq", owner_dev))
    global_tiles = jnp.stack(global_list, axis=1)
    random_three = random_table.reshape(shards, query_blocks, RAND)
    slot_plans = []
    pieces = []
    for slot_num in range(RAND):
        slot_plan = request_plan(random_three[:, :, slot_num], this_shard, query_blocks)
        received = lax.all_to_all(
            serve_tiles(own_blocks, slot_plan), "seq", split_axis=1, concat_axis=1, tiled=True
        )
        pieces.append(pick_tiles(received, slot_plan))
        slot_plans.append(slot_plan)
    fetched = jnp.stack(pieces, axis=2)
    spread_global = jnp.broadcast_to(global_tiles[:, None], (2, query_blocks, GLOB, BLK, kwidth))
    all_tiles = jnp.concatenate([window, spread_global, fetched], axis=2)
    base_ids = this_shard * query_blocks + jnp.arange(query_blocks, dtype=jnp.int32)
    window_ids = base_ids[:, None] + jnp.arange(-1, 2, dtype=jnp.int32)[None, :]
    my_random = lax.dynamic_index_in_dim(random_three, this_shard, 0, keepdims=False)
    tile_ids = jnp.concatenate(
        [window_ids, jnp.broadcast_to(global_ids[None, :], (query_blocks, GLOB)), my_random], axis=1
    )
    key_live = token_live(tile_ids, pad_sizes, query_blocks, shard_tokens, total_blocks)
    query_grad, key_terms, value_terms = block_backward(
        query_rows.reshape(query_blocks, BLK, qwidth),
        grad_rows.reshape(query_blocks, BLK, qwidth),
        all_tiles[0],
        all_tiles[1],
        key_live,
    )
    contrib = jnp.stack([key_terms, value_terms])
    local_sum = contrib[:, :, 1]
    local_sum = local_sum + jnp.pad(contrib[:, 1:, 0], ((0, 0), (0, 1), (0, 0), (0, 0)))
    local_sum = local_sum + jnp.pad(contrib[:, :-1, 2], ((0, 0), (1, 0), (0, 0), (0, 0)))
    edge_out = jnp.concatenate([contrib[:, 0, 0], contrib[:, query_blocks - 1, 2]], axis=1)
    edge_in = extended_2(edge_out.astype(jnp.bfloat16), (("seq", 1),), BLK).astype(edge_out.dtype)
    local_sum = local_sum.at[:, 0].add(edge_in[:, :BLK])
    local_sum = local_sum.at[:, query_blocks - 1].add(edge_in[:, 3 * BLK :])
    global_part = jnp.sum(contrib[:, :, 3:near], axis=1)
    global_total = lax.psum(global_part, "seq")
    global_pick = (
        (global_ids[:, None] // query_blocks == this_shard)
        & (global_ids[:, None] % query_blocks == jnp.arange(query_blocks, dtype=jnp.int32)[None, :])
    ).astype(jnp.float32)
    local_sum = local_sum + jnp.einsum(
        "gq,xgsk->xqsk", global_pick, global_total, precision=lax.Precision.HIGHEST
    )
    random_terms = contrib[:, :, near:].astype(jnp.bfloat16)
    for slot_num in range(RAND):
        returned = lax.all_to_all(
            place_terms(random_terms[:, :, slot_num], slot_plans[slot_num]),
            "seq",
            split_axis=1,
            concat_axis=1,
            tiled=True,
        )
        local_sum = local_sum + absorb_terms(returned, slot_plans[slot_num], query_blocks)
    key_grad = local_sum[0].reshape(shard_tokens, kwidth).astype(jnp.bfloat16)
    value_grad = local_sum[1].reshape(shard_tokens, kwidth).astype(jnp.bfloat16)
    query_low = query_grad.reshape(shard_tokens, qwidth).astype(jnp.bfloat16)
    packed = jnp.concatenate([query_low, key_grad, value_grad], axis=-1)
    handed = from_behind(packed, "section", -1)
    return (
        handed[None, :, :qwidth],
        handed[None, :, qwidth : qwidth + kwidth],
        handed[None, :, qwidth + kwidth :],
    )


def solution(mesh):
    in_specs = (
        P("section", "seq", None),
        P("section", "seq", None),
        P("section", "seq", None),
        P("section", "seq", None),
        P("section", None, None),
        P("section", None),
        P("section", None),
    )
    out_specs = (P("section", "seq", None), P("section", "seq", None), P("section", "seq", None))
    return jax.shard_map(body, mesh=mesh, in_specs=in_specs, out_specs=out_specs, check_vma=False)
```

profile of v0, /device:TPU:1, one launch (start us, length us, event | category | flops | bytes accessed | tf_op | source)
XLA Modules:
  0.0 463.5 jit_solution(16679181156214838141)
XLA Ops:
  9.2 4.0 collective-permute-start
  17.7 6.4 %all-to-all-start = ((bf16[2,8,1,64,512]{4,3,0,2,1:T(8,128)(2,1)}), bf16[2,8,1,64,512]{4,3,0,2,1:T(8,128)(2,1)S(1)}, u32[]{:S(2)}, u32[]{:S(2)}) async-start(bf16[2,8,1,64,512]{4,3,0,2,1:T(8,128)(2,1)} %fusion.54), calls=%async_computation | async-start | bytes 2097152 | tf_op jit(solution)/shard_map/all_to_all | solution.py:196
  35.6 15.4 %all-to-all-done = bf16[2,8,1,64,512]{4,3,0,2,1:T(8,128)(2,1)S(1)} async-done(((bf16[2,8,1,64,512]{4,3,0,2,1:T(8,128)(2,1)}), bf16[2,8,1,64,512]{4,3,0,2,1:T(8,128)(2,1)S(1)}, u32[]{:S(2)}, u32[]{:S(2)}) %all-to-all-start) | async-done | bytes 1048608 | tf_op jit(solution)/shard_map/all_to_all | solution.py:196
  51.1 5.3 %all-to-all-start.1 = ((bf16[2,8,1,64,512]{4,3,0,2,1:T(8,128)(2,1)}), bf16[2,8,1,64,512]{4,3,0,2,1:T(8,128)(2,1)S(1)}, u32[]{:S(2)}, u32[]{:S(2)}) async-start(bf16[2,8,1,64,512]{4,3,0,2,1:T(8,128)(2,1)} %fusion.53), calls=%async_computation.1 | async-start | bytes 2097152 | tf_op jit(solution)/shard_map/all_to_all | solution.py:196
  57.9 2.4 fusion.52
  60.3 21.6 %all-to-all-done.1 = bf16[2,8,1,64,512]{4,3,0,2,1:T(8,128)(2,1)S(1)} async-done(((bf16[2,8,1,64,512]{4,3,0,2,1:T(8,128)(2,1)}), bf16[2,8,1,64,512]{4,3,0,2,1:T(8,128)(2,1)S(1)}, u32[]{:S(2)}, u32[]{:S(2)}) %all-to-all-start.1) | async-done | bytes 1048608 | tf_op jit(solution)/shard_map/all_to_all | solution.py:196
  82.0 4.8 %all-to-all-start.2 = ((bf16[2,8,1,64,512]{4,3,0,2,1:T(8,128)(2,1)}), bf16[2,8,1,64,512]{4,3,0,2,1:T(8,128)(2,1)}, u32[]{:S(2)}, u32[]{:S(2)}) async-start(bf16[2,8,1,64,512]{4,3,0,2,1:T(8,128)(2,1)} %fusion.52), calls=%async_computation.2 | async-start | bytes 2097152 | tf_op jit(solution)/shard_map/all_to_all | solution.py:196
  87.4 3.6 copy.201
  95.4 21.6 %all-reduce.8.cloned.1.call-done = (bf16[2,1,64,512]{3,2,1,0:T(8,128)(2,1)}, bf16[2,1,64,512]{3,2,1,0:T(8,128)(2,1)}) async-done(((bf16[2,1,64,512]{3,2,1,0:T(8,128)(2,1)}, bf16[2,1,64,512]{3,2,1,0:T(8,128)(2,1)}), (bf16[2,1,64,512]{3,2,1,0:T(8,128)(2,1)}, bf16[2,1,64,512]{3,2,1,0:T(8,128)(2,1)})) %all-reduce.8.cloned.1.call-update) | async-done | bytes 262160 | tf_op jit(solution)/shard_map/psum | solution.py:28
  127.2 4.0 fusion.130
  131.2 2.1 reshape_squeeze.12
  133.2 2.1 copy.158
  135.4 4.0 reshape_squeeze.13
  139.4 3.5 copy.160
  142.8 77.5 %while.17 = (s32[]{:T(128)}, bf16[4,4,64,8,128]{4,2,3,1,0:T(8,128)(2,1)}, f32[4,4,8,64,128]{4,3,2,1,0:T(8,128)}, f32[4,4,8,64,128]{4,3,2,1,0:T(8,128)}, bf16[4,4...) while((s32[]{:T(128)}, ...), condition=%wide.region_16.18_spmd.clone, body=%wide.region_12.17_spmd.clone.sunk | while | flops 1633945600 | bytes 56234432 | solution.py:90
  144.2 2.1 bitcast_reduce_fusion.2
  146.3 2.2 fusion.166
  148.6 3.6 fusion.171
  152.2 2.9 fusion.167
  155.1 3.0 fusion.168
  160.1 2.1 fusion.169
  163.6 2.1 bitcast_reduce_fusion.2
  165.7 2.2 fusion.166
  168.0 3.5 fusion.171
  171.5 2.9 fusion.167
  174.4 3.0 fusion.168
  179.5 2.1 fusion.169
  183.0 2.1 bitcast_reduce_fusion.2
  185.1 2.2 fusion.166
  187.4 3.6 fusion.171
  190.9 2.9 fusion.167
  193.9 3.0 fusion.168
  198.9 2.1 fusion.169
  202.4 2.1 bitcast_reduce_fusion.2
  204.5 2.2 fusion.166
  206.7 3.6 fusion.171
  210.3 2.9 fusion.167
  213.2 3.0 fusion.168
  218.2 2.1 fusion.169
  220.3 7.8 %copy.163 = f32[4,8,64,4,128]{4,3,2,0,1:T(4,128)} copy(f32[4,8,64,4,128]{4,2,1,0,3:T(8,128)} %bitcast.563) | data formatting | bytes 8388608 | tf_op jit(solution)/shard_map/transpose | solution.py:95
  228.1 5.5 %stack_reshape.6 = f32[1,4,8,64,512]{4,3,0,1,2:T(8,128)} reshape(f32[4,8,64,4,128]{4,3,2,0,1:T(4,128)} %copy.163) | data formatting | bytes 8388608 | tf_op jit(solution)/shard_map/stack;reshape | solution.py:218
  233.6 5.0 %constant_dynamic-update-slice_fusion.3 = f32[2,4,8,64,512]{4,3,0,1,2:T(8,128)} fusion(f32[1,4,8,64,512]{4,3,0,1,2:T(8,128)} %stack_reshape.6), kind=kLoop, calls=%fused_computation.124 | loop fusion | bytes 8388608
  238.6 5.6 %copy.164 = f32[4,8,64,4,128]{4,3,2,0,1:T(4,128)} copy(f32[4,8,64,4,128]{4,2,1,0,3:T(8,128)S(1)} %bitcast.564) | data formatting | bytes 8388608 | tf_op jit(solution)/shard_map/transpose | solution.py:96
  244.1 5.5 %stack_reshape.7 = f32[1,4,8,64,512]{4,3,0,1,2:T(8,128)} reshape(f32[4,8,64,4,128]{4,3,2,0,1:T(4,128)} %copy.164) | data formatting | bytes 8388608 | tf_op jit(solution)/shard_map/stack;reshape | solution.py:218
  249.6 4.8 %constant_dynamic-update-slice_fusion.2 = f32[2,4,8,64,512]{4,3,0,1,2:T(8,128)} fusion(f32[2,4,8,64,512]{4,3,0,1,2:T(8,128)} %constant_dynamic-update-slice_fusion.3, f32[1,4,8,64,512]{4,3,0,1,2:T(8,128)} %stack_reshape.7), kind=kLoop, calls=%fused_computation.123 | loop fusion | bytes 8388608 | tf_op jit(solution)/shard_map/stack | solution.py:218
  254.4 4.0 convert.13
  262.9 3.7 all-to-all-start.3
  268.6 22.3 %all-to-all-done.3 = bf16[2,8,1,64,512]{4,3,0,2,1:T(8,128)(2,1)S(1)} async-done(((bf16[2,8,1,64,512]{4,3,0,2,1:T(8,128)(2,1)}), bf16[2,8,1,64,512]{4,3,0,2,1:T(8,128)(2,1)S(1)}, u32[]{:S(2)}, u32[]{:S(2)}) %all-to-all-start.3) | async-done | bytes 1048608 | tf_op jit(solution)/shard_map/all_to_all | solution.py:237
  290.9 5.1 %all-to-all-start.4 = ((bf16[2,8,1,64,512]{4,3,0,2,1:T(8,128)(2,1)}), bf16[2,8,1,64,512]{4,3,0,2,1:T(8,128)(2,1)}, u32[]{:S(2)}, u32[]{:S(2)}) async-start(bf16[2,8,1,64,512]{4,3,0,2,1:T(8,128)(2,1)} %copy.173), calls=%async_computation.4 | async-start | bytes 2097152 | tf_op jit(solution)/shard_map/all_to_all | solution.py:237
  301.3 19.4 %all-to-all-done.4 = bf16[2,8,1,64,512]{4,3,0,2,1:T(8,128)(2,1)} async-done(((bf16[2,8,1,64,512]{4,3,0,2,1:T(8,128)(2,1)}), bf16[2,8,1,64,512]{4,3,0,2,1:T(8,128)(2,1)}, u32[]{:S(2)}, u32[]{:S(2)}) %all-to-all-start.4) | async-done | bytes 1048608 | tf_op jit(solution)/shard_map/all_to_all | solution.py:237
  320.6 5.1 %all-to-all-start.5 = ((bf16[2,8,1,64,512]{4,3,0,2,1:T(8,128)(2,1)}), bf16[2,8,1,64,512]{4,3,0,2,1:T(8,128)(2,1)}, u32[]{:S(2)}, u32[]{:S(2)}) async-start(bf16[2,8,1,64,512]{4,3,0,2,1:T(8,128)(2,1)} %copy.176), calls=%async_computation.5 | async-start | bytes 2097152 | tf_op jit(solution)/shard_map/all_to_all | solution.py:237
  327.9 3.7 collective-permute-start.2
  334.1 2.5 fusion.48
  336.6 4.3 copy.162
  340.9 2.8 convert_element_type.53
  346.5 2.9 copy.167
  350.6 6.1 %scatter-add.9 = f32[2,4,64,512]{3,1,2,0:T(4,128)} dynamic-update-slice(f32[2,4,64,512]{3,1,2,0:T(4,128)} %copy.167, f32[2,1,64,512]{3,1,2,0:T(1,128)S(1)} %copy_add_fusion, s32[]{:T(128)} %constant.241.clone.1, s32[]{:T(128)} %constant.245.clone.1, s32[]{:T(128)} %constant.241.clone.1, s32[]{:T(128)} %constant.241.clone.1) | dynamic-update-slice | bytes 524292 | tf_op jit(solution)/shard_map/scatter-add | solution.py:225
  356.8 54.0 %all-reduce.6.cloned.1.call-done = f32[2,2,64,512]{3,1,2,0:T(2,128)} async-done(((f32[2,2,64,512]{3,1,2,0:T(2,128)}), f32[2,2,64,512]{3,1,2,0:T(2,128)}) %all-reduce.6.cloned.1.call-update) | async-done | bytes 524304 | tf_op jit(solution)/shard_map/psum | solution.py:227
  410.8 2.6 fusion.45
  413.4 2.1 fusion.44
  415.5 3.0 fusion.43
  418.6 2.3 fusion.46
  421.4 2.5 collective-permute-start.4
  424.0 30.4 %collective-permute-done.4 = bf16[256,5120]{1,0:T(8,128)(2,1)S(1)} collective-permute-done((bf16[256,5120]{1,0:T(8,128)(2,1)S(1)}, bf16[256,5120]{1,0:T(8,128)(2,1)S(1)}, u32[]{:S(2)}, u32[]{:S(2)}) %collective-permute-start.4) | collective-permute-done | bytes 2621472 | tf_op jit(solution)/shard_map/ppermute | solution.py:34
  (182 shorter events, 65.7 us)
Async XLA Ops:
  7.2 17.0 %copy-start.20 = (s32[1,2]{1,0:T(1,128)S(1)}, s32[1,2]{1,0:T(1,128)}, u32[]{:S(2)}) copy-start(s32[1,2]{1,0:T(1,128)} %param.20) | copy-start | bytes 28
  9.2 83.6 %collective-permute-start = (bf16[2,64,512]{2,1,0:T(8,128)(2,1)S(1)}, bf16[2,64,512]{2,1,0:T(8,128)(2,1)S(1)}, u32[]{:S(2)}, u32[]{:S(2)}) collective-permute-start(bf16[2,64,512]{2,1,0:T(8,128)(2,1)S(1)} %get-tuple-element.194), channel_id=1, source_target_pairs={{0,1},{1,2},{2,3},{3,4},{4,5},{5,6},{6,7},{8,9},{9,10},{10,11},{11... | collective-permute-start | bytes 393224 | tf_op jit(solution)/shard_map/ppermute | solution.py:20
  13.1 79.7 %collective-permute-start.1 = (bf16[2,64,512]{2,1,0:T(8,128)(2,1)S(1)}, bf16[2,64,512]{2,1,0:T(8,128)(2,1)S(1)}, u32[]{:S(2)}, u32[]{:S(2)}) collective-permute-start(bf16[2,64,512]{2,1,0:T(8,128)(2,1)S(1)} %get-tuple-element.195), channel_id=1, source_target_pairs={{1,0},{2,1},{3,2},{4,3},{5,4},{6,5},{7,6},{9,8},{10,9},{11,10},{12... | collective-permute-start | bytes 393224 | tf_op jit(solution)/shard_map/ppermute | solution.py:21
  15.9 15.9 %copy-start.5 = (pred[8]{0:T(512)(128)(4,1)}, pred[8]{0:T(512)(128)(4,1)S(1)}, u32[]{:S(2)}) copy-start(pred[8]{0:T(512)(128)(4,1)S(1)} %get-tuple-element.173) | copy-start | bytes 28
  15.9 15.9 %copy-start.11 = (s32[8]{0:T(128)}, s32[8]{0:T(128)S(1)}, u32[]{:S(2)}) copy-start(s32[8]{0:T(128)S(1)} %fusion.79) | copy-start | bytes 100
  17.7 33.3 %all-to-all-start = ((bf16[2,8,1,64,512]{4,3,0,2,1:T(8,128)(2,1)}), bf16[2,8,1,64,512]{4,3,0,2,1:T(8,128)(2,1)S(1)}, u32[]{:S(2)}, u32[]{:S(2)}) async-start(bf16[2,8,1,64,512]{4,3,0,2,1:T(8,128)(2,1)} %fusion.54), calls=%async_computation | async-start | bytes 2097152 | tf_op jit(solution)/shard_map/all_to_all | solution.py:196
  24.1 92.9 %all-reduce.8.cloned.1.call-start = ((), (), s32[]{:S(2)}) async-start(), calls=%async_computation.7 | async-start | bytes 524288 | tf_op jit(solution)/shard_map/psum | solution.py:28
  30.8 20.3 %copy-start.7 = (pred[8]{0:T(512)(128)(4,1)}, pred[8]{0:T(512)(128)(4,1)S(1)}, u32[]{:S(2)}) copy-start(pred[8]{0:T(512)(128)(4,1)S(1)} %get-tuple-element.171) | copy-start | bytes 28
  30.8 20.2 %copy-start.13 = (s32[8]{0:T(128)}, s32[8]{0:T(128)S(1)}, u32[]{:S(2)}) copy-start(s32[8]{0:T(128)S(1)} %fusion.83) | copy-start | bytes 100
  31.8 24.8 %copy-start.22 = (s32[1,8]{1,0:T(1,128)S(1)}, s32[1,8]{1,0:T(1,128)}, u32[]{:S(2)}) copy-start(s32[1,8]{1,0:T(1,128)} %param.21) | copy-start | bytes 100
  32.6 27.7 %copy-start.9 = (pred[8]{0:T(512)(128)(4,1)}, pred[8]{0:T(512)(128)(4,1)S(1)}, u32[]{:S(2)}) copy-start(pred[8]{0:T(512)(128)(4,1)S(1)} %get-tuple-element.169) | copy-start | bytes 28
  32.7 27.7 %copy-start.15 = (s32[8]{0:T(128)}, s32[8]{0:T(128)S(1)}, u32[]{:S(2)}) copy-start(s32[8]{0:T(128)S(1)} %fusion.87) | copy-start | bytes 100
  51.1 30.9 %all-to-all-start.1 = ((bf16[2,8,1,64,512]{4,3,0,2,1:T(8,128)(2,1)}), bf16[2,8,1,64,512]{4,3,0,2,1:T(8,128)(2,1)S(1)}, u32[]{:S(2)}, u32[]{:S(2)}) async-start(bf16[2,8,1,64,512]{4,3,0,2,1:T(8,128)(2,1)} %fusion.53), calls=%async_computation.1 | async-start | bytes 2097152 | tf_op jit(solution)/shard_map/all_to_all | solution.py:196
  82.0 42.5 %all-to-all-start.2 = ((bf16[2,8,1,64,512]{4,3,0,2,1:T(8,128)(2,1)}), bf16[2,8,1,64,512]{4,3,0,2,1:T(8,128)(2,1)}, u32[]{:S(2)}, u32[]{:S(2)}) async-start(bf16[2,8,1,64,512]{4,3,0,2,1:T(8,128)(2,1)} %fusion.52), calls=%async_computation.2 | async-start | bytes 2097152 | tf_op jit(solution)/shard_map/all_to_all | solution.py:196
  87.4 3.6 copy-start.3
  148.6 3.6 copy-start.4
  168.0 3.6 copy-start.4
  187.3 3.6 copy-start.4
  206.7 3.6 copy-start.4
  233.6 5.0 %copy-start.1 = (f32[4,4,8,64,128]{4,3,2,1,0:T(8,128)S(1)}, f32[4,4,8,64,128]{4,3,2,1,0:T(8,128)}, u32[]{:S(2)}) copy-start(f32[4,4,8,64,128]{4,3,2,1,0:T(8,128)} %get-tuple-element.79) | copy-start | bytes 12582916
  258.4 2.0 copy-start
  260.4 0.6 copy-start.19
  260.5 6.2 %copy-start.18 = (s32[4]{0:T(128)S(1)}, s32[4]{0:T(128)}, u32[]{:S(2)}) copy-start(s32[4]{0:T(128)} %get-tuple-element.206) | copy-start | bytes 52
  262.9 33.1 %copy-start.21 = (s32[1,2]{1,0:T(1,128)S(1)}, s32[1,2]{1,0:T(1,128)}, u32[]{:S(2)}) copy-start(s32[1,2]{1,0:T(1,128)} %param.20) | copy-start | bytes 28
  262.9 28.0 %all-to-all-start.3 = ((bf16[2,8,1,64,512]{4,3,0,2,1:T(8,128)(2,1)}), bf16[2,8,1,64,512]{4,3,0,2,1:T(8,128)(2,1)S(1)}, u32[]{:S(2)}, u32[]{:S(2)}) async-start(bf16[2,8,1,64,512]{4,3,0,2,1:T(8,128)(2,1)} %copy.170), calls=%async_computation.3 | async-start | bytes 2097152 | tf_op jit(solution)/shard_map/all_to_all | solution.py:237
  266.6 29.6 %copy-start.17 = (s32[4]{0:T(128)S(1)}, s32[4]{0:T(128)}, u32[]{:S(2)}) copy-start(s32[4]{0:T(128)} %get-tuple-element.204) | copy-start | bytes 52
  290.9 10.3 %copy-start.2 = (bf16[2,8,1,64,512]{4,3,0,2,1:T(8,128)(2,1)}, bf16[2,8,1,64,512]{4,3,0,2,1:T(8,128)(2,1)S(1)}, u32[]{:S(2)}) copy-start(bf16[2,8,1,64,512]{4,3,0,2,1:T(8,128)(2,1)S(1)} %all-to-all-done.3) | copy-start | bytes 3145732
  290.9 29.7 %all-to-all-start.4 = ((bf16[2,8,1,64,512]{4,3,0,2,1:T(8,128)(2,1)}), bf16[2,8,1,64,512]{4,3,0,2,1:T(8,128)(2,1)}, u32[]{:S(2)}, u32[]{:S(2)}) async-start(bf16[2,8,1,64,512]{4,3,0,2,1:T(8,128)(2,1)} %copy.173), calls=%async_computation.4 | async-start | bytes 2097152 | tf_op jit(solution)/shard_map/all_to_all | solution.py:237
  320.6 97.9 %all-to-all-start.5 = ((bf16[2,8,1,64,512]{4,3,0,2,1:T(8,128)(2,1)}), bf16[2,8,1,64,512]{4,3,0,2,1:T(8,128)(2,1)}, u32[]{:S(2)}, u32[]{:S(2)}) async-start(bf16[2,8,1,64,512]{4,3,0,2,1:T(8,128)(2,1)} %copy.176), calls=%async_computation.5 | async-start | bytes 2097152 | tf_op jit(solution)/shard_map/all_to_all | solution.py:237
  325.7 85.0 %all-reduce.6.cloned.1.call-start = ((), (), s32[]{:S(2)}) async-start(), calls=%async_computation.6 | async-start | bytes 1048576 | tf_op jit(solution)/shard_map/psum | solution.py:227
  327.9 15.9 %collective-permute-start.2 = (bf16[2,64,512]{2,1,0:T(8,128)(2,1)S(1)}, bf16[2,64,512]{2,1,0:T(8,128)(2,1)}, u32[]{:S(2)}, u32[]{:S(2)}) collective-permute-start(bf16[2,64,512]{2,1,0:T(8,128)(2,1)S(1)} %get-tuple-element.184), channel_id=1, source_target_pairs={{0,1},{1,2},{2,3},{3,4},{4,5},{5,6},{6,7},{8,9},{9,10},{10,11},{11... | collective-permute-start | bytes 393224 | tf_op jit(solution)/shard_map/ppermute | solution.py:20
  331.6 12.2 %collective-permute-start.3 = (bf16[2,64,512]{2,1,0:T(8,128)(2,1)}, bf16[2,64,512]{2,1,0:T(8,128)(2,1)}, u32[]{:S(2)}, u32[]{:S(2)}) collective-permute-start(bf16[2,64,512]{2,1,0:T(8,128)(2,1)} %get-tuple-element.185), channel_id=1, source_target_pairs={{1,0},{2,1},{3,2},{4,3},{5,4},{6,5},{7,6},{9,8},{10,9},{11,10},{12... | collective-permute-start | bytes 393224 | tf_op jit(solution)/shard_map/ppermute | solution.py:21
  343.7 69.7 %copy-start.6 = (pred[8]{0:T(512)(128)(4,1)S(1)}, pred[8]{0:T(512)(128)(4,1)}, u32[]{:S(2)}) copy-start(pred[8]{0:T(512)(128)(4,1)} %copy-done.5) | copy-start | bytes 28
  343.8 69.7 %copy-start.12 = (s32[8]{0:T(128)S(1)}, s32[8]{0:T(128)}, u32[]{:S(2)}) copy-start(s32[8]{0:T(128)} %copy-done.11) | copy-start | bytes 100
  349.3 66.1 %copy-start.8 = (pred[8]{0:T(512)(128)(4,1)S(1)}, pred[8]{0:T(512)(128)(4,1)}, u32[]{:S(2)}) copy-start(pred[8]{0:T(512)(128)(4,1)} %copy-done.7) | copy-start | bytes 28
  349.4 66.1 %copy-start.14 = (s32[8]{0:T(128)S(1)}, s32[8]{0:T(128)}, u32[]{:S(2)}) copy-start(s32[8]{0:T(128)} %copy-done.13) | copy-start | bytes 100
  356.8 61.8 %copy-start.10 = (pred[8]{0:T(512)(128)(4,1)S(1)}, pred[8]{0:T(512)(128)(4,1)}, u32[]{:S(2)}) copy-start(pred[8]{0:T(512)(128)(4,1)} %copy-done.9) | copy-start | bytes 28
  356.8 61.8 %copy-start.16 = (s32[8]{0:T(128)S(1)}, s32[8]{0:T(128)}, u32[]{:S(2)}) copy-start(s32[8]{0:T(128)} %copy-done.15) | copy-start | bytes 100
  421.4 33.0 %collective-permute-start.4 = (bf16[256,5120]{1,0:T(8,128)(2,1)S(1)}, bf16[256,5120]{1,0:T(8,128)(2,1)S(1)}, u32[]{:S(2)}, u32[]{:S(2)}) collective-permute-start(bf16[256,5120]{1,0:T(8,128)(2,1)S(1)} %pad_maximum_fusion), channel_id=1, source_target_pairs={{8,0},{16,8},{24,16},{0,24},{9,1},{17,9},{25,17},{1,25},{10,2},{18... | collective-permute-start | bytes 7864328 | tf_op jit(solution)/shard_map/ppermute | solution.py:34
Sparse Core Ops, SparseCore 0:
  30.9 86.1 all-reduce.7
  334.3 76.4 all-reduce.5
where the time goes:
time: 465 us; the launch traced here: 463 us
  waiting for transfers between devices  185 us (40%)
  local copies, waits for them, and re-layouts  112 us (24%)
  matrix products  73.1 us (16%)
  starting transfers between devices  43.5 us (9%)
  other arithmetic  30.4 us (7%)
  between operations  19.9 us (4%)
    psum x1, waiting for transfers between devices, body(): global_total = lax.psum(global_part, 'seq')  54 us
    all_to_all x3, waiting for transfers between devices, body(): lax.all_to_all(place_terms(random_terms[:, :, slot_num], slot_plans[slot_...  41.7 us
    all_to_all x3, waiting for transfers between devices, body(): lax.all_to_all(serve_tiles(own_blocks, slot_plan), 'seq', split_axis=1, c...  37.1 us
    ppermute x1, waiting for transfers between devices, from_behind(): return lax.ppermute(block, axis, route)  30.4 us
    unnamed x56, local copies, waits for them, and re-layouts  24.8 us
    psum x1, waiting for transfers between devices, broadcast(): return lax.psum(jnp.where(mine, array, jnp.zeros_like(array)), axis)  21.6 us
    all_to_all x3, starting transfers between devices, body(): lax.all_to_all(serve_tiles(own_blocks, slot_plan), 'seq', split_axis=1, c...  16.5 us
    another operation x3, local copies, waits for them, and re-layouts, body(): contrib = jnp.stack([key_terms, value_terms])  15.8 us
  transfers between devices with their start and end apart: 13, of which 7 were waited for; matrix products, arithmetic and copies ran while one was open for 15% of the time, Pallas kernels for 0%

commit v1 on v0

--- a/solution.py
+++ b/solution.py
@@ -1,3 +1,4 @@
+import functools
 import math
 import jax
 import jax.numpy as jnp
@@ -8,6 +9,41 @@
 BLK = 64
 GLOB = 2
 RAND = 3
+
+
+def group_goods(raw, array_dim, load):
+    m_next = raw.shape
+    return jnp.moveaxis(
+        raw.reshape(*m_next[:array_dim], load, m_next[array_dim] // load, *m_next[array_dim + 1 :]),
+        array_dim,
+        0,
+    )
+
+
+def match_stages_all(frame, d0):
+    frame = jnp.moveaxis(frame, 0, d0)
+    outcome_arr = frame.shape
+    return frame.reshape(
+        *outcome_arr[:d0], outcome_arr[d0] * outcome_arr[d0 + 1], *outcome_arr[d0 + 2 :]
+    )
+
+
+def match_surface(chunk, along_axis, patch, content):
+    f_next, x_new = (lax.axis_size(along_axis), lax.axis_index(along_axis))
+    passed = group_goods(chunk, patch, f_next)
+    by_place = [passed[x_new]]
+    for jj in [*range(1, f_next)]:
+        block_next = passed[x_new ^ jj]
+        by_place.append(
+            lax.ppermute(
+                block_next, axis_name=along_axis, perm=[(c, c ^ jj) for c in range(f_next)]
+            )
+        )
+    passed = jnp.stack(by_place)[x_new ^ jnp.arange(f_next)]
+    return match_stages_all(passed, content)
+
+
+mark_fields_here = functools.partial(match_surface, along_axis="seq", patch=1, content=1)
 
 
 def extended_2(array, sides, width):
@@ -234,13 +270,7 @@
     )
     random_terms = contrib[:, :, near:].astype(jnp.bfloat16)
     for slot_num in range(RAND):
-        returned = lax.all_to_all(
-            place_terms(random_terms[:, :, slot_num], slot_plans[slot_num]),
-            "seq",
-            split_axis=1,
-            concat_axis=1,
-            tiled=True,
-        )
+        returned = mark_fields_here(place_terms(random_terms[:, :, slot_num], slot_plans[slot_num]))
         local_sum = local_sum + absorb_terms(returned, slot_plans[slot_num], query_blocks)
     key_grad = local_sum[0].reshape(shard_tokens, kwidth).astype(jnp.bfloat16)
     value_grad = local_sum[1].reshape(shard_tokens, kwidth).astype(jnp.bfloat16)

time: 465 us -> 436 us (0.938); the launches traced: 463 us -> 428 us
  waiting for transfers between devices: 185 us -> 98.4 us
  starting transfers between devices: 43.5 us -> 70.9 us
  local copies, waits for them, and re-layouts: 112 us -> 139 us
    psum x1, waiting for transfers between devices: 54 us -> 0.01 us  [body(): global_total = lax.psum(global_part, 'seq')]
    all_to_all x3 -> x0, waiting for transfers between devices: 41.7 us -> none  [body(): lax.all_to_all(place_terms(random_terms[:, :, slot_num], slot_plans[slot_...]
    ppermute x0 -> x21, starting transfers between devices: none -> 38.6 us  [match_surface(): lax.ppermute(block_next, axis_name=along_axis, perm=[(c, c ^ jj) for c in...]
    unnamed x56 -> x89, local copies, waits for them, and re-layouts: 24.8 us -> 47.3 us
    all_to_all x3 -> x0, starting transfers between devices: 13.9 us -> none  [body(): lax.all_to_all(place_terms(random_terms[:, :, slot_num], slot_plans[slot_...]
    ppermute x0 -> x21, waiting for transfers between devices: none -> 9.12 us  [match_surface(): lax.ppermute(block_next, axis_name=along_axis, perm=[(c, c ^ jj) for c in...]
    gather x0 -> x3, local copies, waits for them, and re-layouts: none -> 7.89 us  [match_surface(): passed = jnp.stack(by_place)[x_new ^ jnp.arange(f_next)]]
    all_to_all x3, waiting for transfers between devices: 37.1 us -> 32.4 us  [body(): lax.all_to_all(serve_tiles(own_blocks, slot_plan), 'seq', split_axis=1, c...]
  transfers between devices with their start and end apart: 13 -> 31, of which waited for: 7 -> 7; matrix products, arithmetic and copies ran while one was open for 15% -> 19% of each run, Pallas kernels for 0% -> 0%
where the time goes in v1:
time: 436 us; the launch traced here: 428 us
  local copies, waits for them, and re-layouts  139 us (32%)
  waiting for transfers between devices  98.4 us (23%)
  starting transfers between devices  70.9 us (16%)
  matrix products  69.4 us (16%)
  other arithmetic  29.6 us (7%)
  between operations  20.3 us (5%)
    unnamed x89, local copies, waits for them, and re-layouts  47.3 us
    ppermute x21, starting transfers between devices, match_surface(): lax.ppermute(block_next, axis_name=along_axis, perm=[(c, c ^ jj) for c in...  38.6 us
    all_to_all x3, waiting for transfers between devices, body(): lax.all_to_all(serve_tiles(own_blocks, slot_plan), 'seq', split_axis=1, c...  32.4 us
    ppermute x1, waiting for transfers between devices, from_behind(): return lax.ppermute(block, axis, route)  30.6 us
    psum x1, waiting for transfers between devices, broadcast(): return lax.psum(jnp.where(mine, array, jnp.zeros_like(array)), axis)  26.2 us
    all_to_all x3, starting transfers between devices, body(): lax.all_to_all(serve_tiles(own_blocks, slot_plan), 'seq', split_axis=1, c...  16.5 us
    another operation x3, local copies, waits for them, and re-layouts, body(): contrib = jnp.stack([key_terms, value_terms])  15.8 us
    dot_general x4, matrix products, one_head(): jnp.einsum('bgqtk,bqgd->btkd', probs_low, grad_one, preferred_element_typ...  14.3 us
  transfers between devices with their start and end apart: 31, of which 7 were waited for; matrix products, arithmetic and copies ran while one was open for 19% of the time, Pallas kernels for 0%

profile of v1, /device:TPU:1, one launch (start us, length us, event | category | flops | bytes accessed | tf_op | source)
XLA Modules:
  0.0 428.1 jit_solution(7219543732797317226)
XLA Ops:
  9.2 4.0 collective-permute-start
  17.7 6.4 %all-to-all-start = ((bf16[2,8,1,64,512]{4,3,0,2,1:T(8,128)(2,1)}), bf16[2,8,1,64,512]{4,3,0,2,1:T(8,128)(2,1)}, u32[]{:S(2)}, u32[]{:S(2)}) async-start(bf16[2,8,1,64,512]{4,3,0,2,1:T(8,128)(2,1)} %fusion.51), calls=%async_computation | async-start | bytes 2097152 | tf_op jit(solution)/shard_map/all_to_all | solution.py:232
  34.9 16.3 %all-to-all-done = bf16[2,8,1,64,512]{4,3,0,2,1:T(8,128)(2,1)} async-done(((bf16[2,8,1,64,512]{4,3,0,2,1:T(8,128)(2,1)}), bf16[2,8,1,64,512]{4,3,0,2,1:T(8,128)(2,1)}, u32[]{:S(2)}, u32[]{:S(2)}) %all-to-all-start) | async-done | bytes 1048608 | tf_op jit(solution)/shard_map/all_to_all | solution.py:232
  51.2 5.3 %all-to-all-start.1 = ((bf16[2,8,1,64,512]{4,3,0,2,1:T(8,128)(2,1)}), bf16[2,8,1,64,512]{4,3,0,2,1:T(8,128)(2,1)S(1)}, u32[]{:S(2)}, u32[]{:S(2)}) async-start(bf16[2,8,1,64,512]{4,3,0,2,1:T(8,128)(2,1)} %fusion.50), calls=%async_computation.1 | async-start | bytes 2097152 | tf_op jit(solution)/shard_map/all_to_all | solution.py:232
  60.6 3.6 copy.224
  65.9 16.1 %all-to-all-done.1 = bf16[2,8,1,64,512]{4,3,0,2,1:T(8,128)(2,1)S(1)} async-done(((bf16[2,8,1,64,512]{4,3,0,2,1:T(8,128)(2,1)}), bf16[2,8,1,64,512]{4,3,0,2,1:T(8,128)(2,1)S(1)}, u32[]{:S(2)}, u32[]{:S(2)}) %all-to-all-start.1) | async-done | bytes 1048608 | tf_op jit(solution)/shard_map/all_to_all | solution.py:232
  82.1 4.8 %all-to-all-start.2 = ((bf16[2,8,1,64,512]{4,3,0,2,1:T(8,128)(2,1)}), bf16[2,8,1,64,512]{4,3,0,2,1:T(8,128)(2,1)S(1)}, u32[]{:S(2)}, u32[]{:S(2)}) async-start(bf16[2,8,1,64,512]{4,3,0,2,1:T(8,128)(2,1)} %fusion.49), calls=%async_computation.2 | async-start | bytes 2097152 | tf_op jit(solution)/shard_map/all_to_all | solution.py:232
  90.7 26.2 %all-reduce.8.cloned.1.call-done = (bf16[2,1,64,512]{3,2,1,0:T(8,128)(2,1)}, bf16[2,1,64,512]{3,2,1,0:T(8,128)(2,1)}) async-done(((bf16[2,1,64,512]{3,2,1,0:T(8,128)(2,1)}, bf16[2,1,64,512]{3,2,1,0:T(8,128)(2,1)}), (bf16[2,1,64,512]{3,2,1,0:T(8,128)(2,1)}, bf16[2,1,64,512]{3,2,1,0:T(8,128)(2,1)})) %all-reduce.8.cloned.1.call-update) | async-done | bytes 262160 | tf_op jit(solution)/shard_map/psum | solution.py:64
  124.6 4.0 fusion.128
  130.6 2.1 copy.184
  132.7 4.0 reshape_squeeze.13
  136.7 3.5 copy.186
  140.2 77.6 %while.17 = (s32[]{:T(128)}, bf16[4,4,64,8,128]{4,2,3,1,0:T(8,128)(2,1)}, f32[4,4,8,64,128]{4,3,2,1,0:T(8,128)}, f32[4,4,8,64,128]{4,3,2,1,0:T(8,128)}, bf16[4,4...) while((s32[]{:T(128)}, ...), condition=%wide.region_16.18_spmd.clone, body=%wide.region_12.17_spmd.clone.sunk | while | flops 1633945600 | bytes 56234432 | solution.py:126
  143.7 2.2 fusion.164
  146.0 3.6 fusion.169
  149.6 2.9 fusion.165
  152.5 3.0 fusion.166
  157.5 2.1 fusion.167
  161.0 2.1 bitcast_reduce_fusion.2
  163.1 2.2 fusion.164
  165.4 3.6 fusion.169
  168.9 2.9 fusion.165
  171.9 3.1 fusion.166
  176.9 2.1 fusion.167
  180.4 2.1 bitcast_reduce_fusion.2
  182.5 2.2 fusion.164
  184.8 3.6 fusion.169
  188.3 2.9 fusion.165
  191.2 3.0 fusion.166
  196.2 2.1 fusion.167
  199.7 2.1 bitcast_reduce_fusion.2
  201.9 2.2 fusion.164
  204.1 3.6 fusion.169
  207.7 2.9 fusion.165
  210.6 3.0 fusion.166
  215.6 2.1 fusion.167
  217.9 7.8 %copy.189 = f32[4,8,64,4,128]{4,3,2,0,1:T(4,128)} copy(f32[4,8,64,4,128]{4,2,1,0,3:T(8,128)} %bitcast.661) | data formatting | bytes 8388608 | tf_op jit(solution)/shard_map/transpose | solution.py:131
  225.7 5.5 %stack_reshape.6 = f32[1,4,8,64,512]{4,3,0,1,2:T(8,128)} reshape(f32[4,8,64,4,128]{4,3,2,0,1:T(4,128)} %copy.189) | data formatting | bytes 8388608 | tf_op jit(solution)/shard_map/stack;reshape | solution.py:254
  231.1 5.1 %constant_dynamic-update-slice_fusion.3 = f32[2,4,8,64,512]{4,3,0,1,2:T(8,128)} fusion(f32[1,4,8,64,512]{4,3,0,1,2:T(8,128)} %stack_reshape.6), kind=kLoop, calls=%fused_computation.169 | loop fusion | bytes 8388608
  236.2 5.5 %copy.190 = f32[4,8,64,4,128]{4,3,2,0,1:T(4,128)} copy(f32[4,8,64,4,128]{4,2,1,0,3:T(8,128)S(1)} %bitcast.662) | data formatting | bytes 8388608 | tf_op jit(solution)/shard_map/transpose | solution.py:132
  241.7 5.5 %stack_reshape.7 = f32[1,4,8,64,512]{4,3,0,1,2:T(8,128)} reshape(f32[4,8,64,4,128]{4,3,2,0,1:T(4,128)} %copy.190) | data formatting | bytes 8388608 | tf_op jit(solution)/shard_map/stack;reshape | solution.py:254
  247.2 4.9 %constant_dynamic-update-slice_fusion.2 = f32[2,4,8,64,512]{4,3,0,1,2:T(8,128)} fusion(f32[2,4,8,64,512]{4,3,0,1,2:T(8,128)} %constant_dynamic-update-slice_fusion.3, f32[1,4,8,64,512]{4,3,0,1,2:T(8,128)} %stack_reshape.7), kind=kLoop, calls=%fused_computation.168 | loop fusion | bytes 8388608 | tf_op jit(solution)/shard_map/stack | solution.py:254
  252.1 4.0 convert.13
  264.9 2.6 slice_bitcast_fusion.3
  273.6 3.2 collective-permute-start.2
  279.6 4.3 %copy.188 = bf16[4,64,4,8,128]{4,3,2,1,0:T(8,128)(2,1)} copy(bf16[4,64,4,8,128]{4,1,3,0,2:T(8,128)(2,1)} %bitcast.577) | data formatting | bytes 4194304 | tf_op jit(solution)/shard_map/convert_element_type | solution.py:277
  283.9 2.8 convert_element_type.53
  289.9 2.1 collective-permute-start.21
  292.0 2.2 collective-permute-start.22
  300.8 2.2 collective-permute-start.11
  304.0 6.2 %collective-permute-start.12 = (bf16[2,1,1,64,512]{4,3,0,2,1:T(8,128)(2,1)}, bf16[2,1,1,64,512]{4,3,0,2,1:T(8,128)(2,1)}, u32[]{:S(2)}, u32[]{:S(2)}) collective-permute-start(bf16[2,1,1,64,512]{4,3,0,2,1:T(8,128)(2,1)} %get-tuple-element.213), channel_id=1, source_target_pairs={{0,2},{1,3},{2,0},{3,1},{4,6},{5,7},{6,4},{7,5},{8,10},{9,11},{10,... | collective-permute-start | bytes 393224 | tf_op jit(solution)/shard_map/ppermute | solution.py:38
  310.2 5.2 %collective-permute-done.22 = bf16[2,1,1,64,512]{4,3,0,2,1:T(8,128)(2,1)S(1)} collective-permute-done((bf16[2,1,1,64,512]{4,3,0,2,1:T(8,128)(2,1)S(1)}, bf16[2,1,1,64,512]{4,3,0,2,1:T(8,128)(2,1)S(1)}, u32[]{:S(2)}, u32[]{:S(2)}) %collective-permute-start.22) | collective-permute-done | bytes 131104 | tf_op jit(solution)/shard_map/ppermute | solution.py:38
  315.5 2.5 collective-permute-start.14
  318.0 5.3 %collective-permute-start.15 = (bf16[2,1,1,64,512]{4,3,0,2,1:T(8,128)(2,1)}, bf16[2,1,1,64,512]{4,3,0,2,1:T(8,128)(2,1)}, u32[]{:S(2)}, u32[]{:S(2)}) collective-permute-start(bf16[2,1,1,64,512]{4,3,0,2,1:T(8,128)(2,1)} %get-tuple-element.210), channel_id=1, source_target_pairs={{0,5},{1,4},{2,7},{3,6},{4,1},{5,0},{6,3},{7,2},{8,13},{9,12},{10,... | collective-permute-start | bytes 393224 | tf_op jit(solution)/shard_map/ppermute | solution.py:38
  327.9 4.5 %collective-permute-start.17 = (bf16[2,1,1,64,512]{4,3,0,2,1:T(8,128)(2,1)}, bf16[2,1,1,64,512]{4,3,0,2,1:T(8,128)(2,1)S(1)}, u32[]{:S(2)}, u32[]{:S(2)}) collective-permute-start(bf16[2,1,1,64,512]{4,3,0,2,1:T(8,128)(2,1)} %get-tuple-element.208), channel_id=1, source_target_pairs={{0,7},{1,6},{2,5},{3,4},{4,3},{5,2},{6,1},{7,0},{8,15},{9,14},{10,... | collective-permute-start | bytes 393224 | tf_op jit(solution)/shard_map/ppermute | solution.py:38
  337.1 3.3 collective-permute-done.15
  343.3 3.7 collective-permute-start.8
  347.6 3.0 gather_fusion.4
  352.3 4.0 collective-permute-start.10
  364.4 3.0 gather_fusion.3
  369.6 6.1 %scatter-add.9 = f32[2,4,64,512]{3,1,2,0:T(4,128)} dynamic-update-slice(f32[2,4,64,512]{3,1,2,0:T(4,128)} %copy.193, f32[2,1,64,512]{3,1,2,0:T(1,128)S(1)} %copy_add_fusion, s32[]{:T(128)} %constant.250.clone.1, s32[]{:T(128)} %constant.254.clone.1, s32[]{:T(128)} %constant.250.clone.1, s32[]{:T(128)} %constant.250.clone.1) | dynamic-update-slice | bytes 524292 | tf_op jit(solution)/shard_map/scatter-add | solution.py:261
  375.8 2.7 fusion.45
  382.8 5.3 %collective-permute-start.25 = (bf16[256,5120]{1,0:T(8,128)(2,1)S(1)}, bf16[256,5120]{1,0:T(8,128)(2,1)S(1)}, u32[]{:S(2)}, u32[]{:S(2)}) collective-permute-start(bf16[256,5120]{1,0:T(8,128)(2,1)S(1)} %pad_maximum_fusion), channel_id=1, source_target_pairs={{8,0},{16,8},{24,16},{0,24},{9,1},{17,9},{25,17},{1,25},{10,2},{18... | collective-permute-start | bytes 7864328 | tf_op jit(solution)/shard_map/ppermute | solution.py:70
  388.1 30.6 %collective-permute-done.25 = bf16[256,5120]{1,0:T(8,128)(2,1)S(1)} collective-permute-done((bf16[256,5120]{1,0:T(8,128)(2,1)S(1)}, bf16[256,5120]{1,0:T(8,128)(2,1)S(1)}, u32[]{:S(2)}, u32[]{:S(2)}) %collective-permute-start.25) | collective-permute-done | bytes 2621472 | tf_op jit(solution)/shard_map/ppermute | solution.py:70
  (256 shorter events, 106.3 us)
Async XLA Ops:
  7.2 17.0 %copy-start.27 = (s32[1,2]{1,0:T(1,128)S(1)}, s32[1,2]{1,0:T(1,128)}, u32[]{:S(2)}) copy-start(s32[1,2]{1,0:T(1,128)} %param.20) | copy-start | bytes 28
  9.2 78.8 %collective-permute-start = (bf16[2,64,512]{2,1,0:T(8,128)(2,1)S(1)}, bf16[2,64,512]{2,1,0:T(8,128)(2,1)S(1)}, u32[]{:S(2)}, u32[]{:S(2)}) collective-permute-start(bf16[2,64,512]{2,1,0:T(8,128)(2,1)S(1)} %get-tuple-element.226), channel_id=1, source_target_pairs={{0,1},{1,2},{2,3},{3,4},{4,5},{5,6},{6,7},{8,9},{9,10},{10,11},{11... | collective-permute-start | bytes 393224 | tf_op jit(solution)/shard_map/ppermute | solution.py:56
  13.1 74.9 %collective-permute-start.1 = (bf16[2,64,512]{2,1,0:T(8,128)(2,1)S(1)}, bf16[2,64,512]{2,1,0:T(8,128)(2,1)S(1)}, u32[]{:S(2)}, u32[]{:S(2)}) collective-permute-start(bf16[2,64,512]{2,1,0:T(8,128)(2,1)S(1)} %get-tuple-element.227), channel_id=1, source_target_pairs={{1,0},{2,1},{3,2},{4,3},{5,4},{6,5},{7,6},{9,8},{10,9},{11,10},{12... | collective-permute-start | bytes 393224 | tf_op jit(solution)/shard_map/ppermute | solution.py:57
  15.9 16.1 %copy-start.12 = (pred[8]{0:T(512)(128)(4,1)}, pred[8]{0:T(512)(128)(4,1)S(1)}, u32[]{:S(2)}) copy-start(pred[8]{0:T(512)(128)(4,1)S(1)} %get-tuple-element.184) | copy-start | bytes 28
  15.9 16.1 %copy-start.18 = (s32[8]{0:T(128)}, s32[8]{0:T(128)S(1)}, u32[]{:S(2)}) copy-start(s32[8]{0:T(128)S(1)} %fusion.70) | copy-start | bytes 100
  17.7 33.4 %all-to-all-start = ((bf16[2,8,1,64,512]{4,3,0,2,1:T(8,128)(2,1)}), bf16[2,8,1,64,512]{4,3,0,2,1:T(8,128)(2,1)}, u32[]{:S(2)}, u32[]{:S(2)}) async-start(bf16[2,8,1,64,512]{4,3,0,2,1:T(8,128)(2,1)} %fusion.51), calls=%async_computation | async-start | bytes 2097152 | tf_op jit(solution)/shard_map/all_to_all | solution.py:232
  24.1 92.8 %all-reduce.8.cloned.1.call-start = ((), (), s32[]{:S(2)}) async-start(), calls=%async_computation.4 | async-start | bytes 524288 | tf_op jit(solution)/shard_map/psum | solution.py:64
  31.1 20.0 %copy-start.14 = (pred[8]{0:T(512)(128)(4,1)}, pred[8]{0:T(512)(128)(4,1)S(1)}, u32[]{:S(2)}) copy-start(pred[8]{0:T(512)(128)(4,1)S(1)} %get-tuple-element.182) | copy-start | bytes 28
  31.6 27.8 %copy-start.16 = (pred[8]{0:T(512)(128)(4,1)}, pred[8]{0:T(512)(128)(4,1)S(1)}, u32[]{:S(2)}) copy-start(pred[8]{0:T(512)(128)(4,1)S(1)} %get-tuple-element.180) | copy-start | bytes 28
  32.0 19.2 %copy-start.20 = (s32[8]{0:T(128)}, s32[8]{0:T(128)S(1)}, u32[]{:S(2)}) copy-start(s32[8]{0:T(128)S(1)} %fusion.74) | copy-start | bytes 100
  32.0 24.4 %copy-start.28 = (s32[1,8]{1,0:T(1,128)S(1)}, s32[1,8]{1,0:T(1,128)}, u32[]{:S(2)}) copy-start(s32[1,8]{1,0:T(1,128)} %param.21) | copy-start | bytes 100
  32.7 27.8 %copy-start.22 = (s32[8]{0:T(128)}, s32[8]{0:T(128)S(1)}, u32[]{:S(2)}) copy-start(s32[8]{0:T(128)S(1)} %fusion.78) | copy-start | bytes 100
  51.2 30.9 %all-to-all-start.1 = ((bf16[2,8,1,64,512]{4,3,0,2,1:T(8,128)(2,1)}), bf16[2,8,1,64,512]{4,3,0,2,1:T(8,128)(2,1)S(1)}, u32[]{:S(2)}, u32[]{:S(2)}) async-start(bf16[2,8,1,64,512]{4,3,0,2,1:T(8,128)(2,1)} %fusion.50), calls=%async_computation.1 | async-start | bytes 2097152 | tf_op jit(solution)/shard_map/all_to_all | solution.py:232
  60.6 3.6 copy-start.3
  82.1 41.1 %all-to-all-start.2 = ((bf16[2,8,1,64,512]{4,3,0,2,1:T(8,128)(2,1)}), bf16[2,8,1,64,512]{4,3,0,2,1:T(8,128)(2,1)S(1)}, u32[]{:S(2)}, u32[]{:S(2)}) async-start(bf16[2,8,1,64,512]{4,3,0,2,1:T(8,128)(2,1)} %fusion.49), calls=%async_computation.2 | async-start | bytes 2097152 | tf_op jit(solution)/shard_map/all_to_all | solution.py:232
  86.9 288.9 %all-reduce.6.cloned.1.call-start = ((), (), s32[]{:S(2)}) async-start(), calls=%async_computation.3 | async-start | bytes 1048576 | tf_op jit(solution)/shard_map/psum | solution.py:263
  146.0 3.6 copy-start.4
  165.3 3.6 copy-start.4
  184.7 3.6 copy-start.4
  204.1 3.6 copy-start.4
  231.1 5.1 %copy-start.2 = (f32[4,4,8,64,128]{4,3,2,1,0:T(8,128)S(1)}, f32[4,4,8,64,128]{4,3,2,1,0:T(8,128)}, u32[]{:S(2)}) copy-start(f32[4,4,8,64,128]{4,3,2,1,0:T(8,128)} %get-tuple-element.79) | copy-start | bytes 12582916
  256.1 2.0 copy-start
  258.0 1.0 copy-start.26
  258.1 2.5 copy-start.25
  263.2 9.0 %copy-start.5 = (bf16[4,2,64,512]{3,2,1,0:T(8,128)(2,1)S(1)}, bf16[4,2,64,512]{3,2,1,0:T(8,128)(2,1)}, u32[]{:S(2)}) copy-start(bf16[4,2,64,512]{3,2,1,0:T(8,128)(2,1)} %get-tuple-element.194) | copy-start | bytes 1572868
  263.2 9.0 %copy-start.24 = (s32[4]{0:T(128)S(1)}, s32[4]{0:T(128)}, u32[]{:S(2)}) copy-start(s32[4]{0:T(128)} %get-tuple-element.240) | copy-start | bytes 52
  269.4 27.2 %collective-permute-start.18 = (bf16[2,1,1,64,512]{4,3,0,2,1:T(8,128)(2,1)}, bf16[2,1,1,64,512]{4,3,0,2,1:T(8,128)(2,1)}, u32[]{:S(2)}, u32[]{:S(2)}) collective-permute-start(bf16[2,1,1,64,512]{4,3,0,2,1:T(8,128)(2,1)} %get-tuple-element.207), channel_id=1, source_target_pairs={{0,1},{1,0},{2,3},{3,2},{4,5},{5,4},{6,7},{7,6},{8,9},{9,8},{10,11... | collective-permute-start | bytes 393224 | tf_op jit(solution)/shard_map/ppermute | solution.py:38
  270.7 28.1 %collective-permute-start.19 = (bf16[2,1,1,64,512]{4,3,0,2,1:T(8,128)(2,1)}, bf16[2,1,1,64,512]{4,3,0,2,1:T(8,128)(2,1)}, u32[]{:S(2)}, u32[]{:S(2)}) collective-permute-start(bf16[2,1,1,64,512]{4,3,0,2,1:T(8,128)(2,1)} %get-tuple-element.206), channel_id=1, source_target_pairs={{0,2},{1,3},{2,0},{3,1},{4,6},{5,7},{6,4},{7,5},{8,10},{9,11},{10,... | collective-permute-start | bytes 393224 | tf_op jit(solution)/shard_map/ppermute | solution.py:38
  270.7 30.1 %collective-permute-start.20 = (bf16[2,1,1,64,512]{4,3,0,2,1:T(8,128)(2,1)}, bf16[2,1,1,64,512]{4,3,0,2,1:T(8,128)(2,1)}, u32[]{:S(2)}, u32[]{:S(2)}) collective-permute-start(bf16[2,1,1,64,512]{4,3,0,2,1:T(8,128)(2,1)} %get-tuple-element.205), channel_id=1, source_target_pairs={{0,3},{1,2},{2,1},{3,0},{4,7},{5,6},{6,5},{7,4},{8,11},{9,10},{10,... | collective-permute-start | bytes 393224 | tf_op jit(solution)/shard_map/ppermute | solution.py:38
  273.6 16.2 %collective-permute-start.2 = (bf16[2,64,512]{2,1,0:T(8,128)(2,1)S(1)}, bf16[2,64,512]{2,1,0:T(8,128)(2,1)S(1)}, u32[]{:S(2)}, u32[]{:S(2)}) collective-permute-start(bf16[2,64,512]{2,1,0:T(8,128)(2,1)S(1)} %get-tuple-element.195), channel_id=1, source_target_pairs={{0,1},{1,2},{2,3},{3,4},{4,5},{5,6},{6,7},{8,9},{9,10},{10,11},{11... | collective-permute-start | bytes 393224 | tf_op jit(solution)/shard_map/ppermute | solution.py:56
  276.8 15.1 %collective-permute-start.3 = (bf16[2,64,512]{2,1,0:T(8,128)(2,1)S(1)}, bf16[2,64,512]{2,1,0:T(8,128)(2,1)}, u32[]{:S(2)}, u32[]{:S(2)}) collective-permute-start(bf16[2,64,512]{2,1,0:T(8,128)(2,1)S(1)} %get-tuple-element.196), channel_id=1, source_target_pairs={{1,0},{2,1},{3,2},{4,3},{5,4},{6,5},{7,6},{9,8},{10,9},{11,10},{12... | collective-permute-start | bytes 393224 | tf_op jit(solution)/shard_map/ppermute | solution.py:57
  286.8 3.1 copy-start.11
  286.8 5.2 %copy-start.10 = (bf16[2,1,1,64,512]{4,3,0,2,1:T(8,128)(2,1)S(1)}, bf16[2,1,1,64,512]{4,3,0,2,1:T(8,128)(2,1)}, u32[]{:S(2)}) copy-start(bf16[2,1,1,64,512]{4,3,0,2,1:T(8,128)(2,1)} %get-tuple-element.203) | copy-start | bytes 393220
  286.8 9.8 %copy-start.9 = (bf16[2,1,1,64,512]{4,3,0,2,1:T(8,128)(2,1)S(1)}, bf16[2,1,1,64,512]{4,3,0,2,1:T(8,128)(2,1)}, u32[]{:S(2)}) copy-start(bf16[2,1,1,64,512]{4,3,0,2,1:T(8,128)(2,1)} %get-tuple-element.202) | copy-start | bytes 393220
  286.8 11.1 %copy-start.6 = (bf16[8,2,1,1,64,512]{5,4,1,0,3,2:T(8,128)(2,1)S(1)}, bf16[8,2,1,1,64,512]{5,4,1,0,3,2:T(8,128)(2,1)}, u32[]{:S(2)}) copy-start(bf16[8,2,1,1,64,512]{5,4,1,0,3,2:T(8,128)(2,1)} %bitcast_dynamic-update-slice_fusion.7) | copy-start | bytes 3145732
  286.8 12.1 %copy-start.8 = (bf16[2,1,1,64,512]{4,3,0,2,1:T(8,128)(2,1)S(1)}, bf16[2,1,1,64,512]{4,3,0,2,1:T(8,128)(2,1)}, u32[]{:S(2)}) copy-start(bf16[2,1,1,64,512]{4,3,0,2,1:T(8,128)(2,1)} %get-tuple-element.201) | copy-start | bytes 393220
  289.9 14.1 %collective-permute-start.21 = (bf16[2,1,1,64,512]{4,3,0,2,1:T(8,128)(2,1)S(1)}, bf16[2,1,1,64,512]{4,3,0,2,1:T(8,128)(2,1)S(1)}, u32[]{:S(2)}, u32[]{:S(2)}) collective-permute-start(bf16[2,1,1,64,512]{4,3,0,2,1:T(8,128)(2,1)S(1)} %copy-done.11), channel_id=1, source_target_pairs={{0,4},{1,5},{2,6},{3,7},{4,0},{5,1},{6,2},{7,3},{8,12},{9,13},{10,... | collective-permute-start | bytes 393224 | tf_op jit(solution)/shard_map/ppermute | solution.py:38
  292.0 23.5 %collective-permute-start.22 = (bf16[2,1,1,64,512]{4,3,0,2,1:T(8,128)(2,1)S(1)}, bf16[2,1,1,64,512]{4,3,0,2,1:T(8,128)(2,1)S(1)}, u32[]{:S(2)}, u32[]{:S(2)}) collective-permute-start(bf16[2,1,1,64,512]{4,3,0,2,1:T(8,128)(2,1)S(1)} %copy-done.10), channel_id=1, source_target_pairs={{0,5},{1,4},{2,7},{3,6},{4,1},{5,0},{6,3},{7,2},{8,13},{9,12},{10,... | collective-permute-start | bytes 393224 | tf_op jit(solution)/shard_map/ppermute | solution.py:38
  296.6 18.9 %collective-permute-start.23 = (bf16[2,1,1,64,512]{4,3,0,2,1:T(8,128)(2,1)S(1)}, bf16[2,1,1,64,512]{4,3,0,2,1:T(8,128)(2,1)S(1)}, u32[]{:S(2)}, u32[]{:S(2)}) collective-permute-start(bf16[2,1,1,64,512]{4,3,0,2,1:T(8,128)(2,1)S(1)} %copy-done.9), channel_id=1, source_target_pairs={{0,6},{1,7},{2,4},{3,5},{4,2},{5,3},{6,0},{7,1},{8,14},{9,15},{10,... | collective-permute-start | bytes 393224 | tf_op jit(solution)/shard_map/ppermute | solution.py:38
  298.9 19.1 %collective-permute-start.24 = (bf16[2,1,1,64,512]{4,3,0,2,1:T(8,128)(2,1)S(1)}, bf16[2,1,1,64,512]{4,3,0,2,1:T(8,128)(2,1)S(1)}, u32[]{:S(2)}, u32[]{:S(2)}) collective-permute-start(bf16[2,1,1,64,512]{4,3,0,2,1:T(8,128)(2,1)S(1)} %copy-done.8), channel_id=1, source_target_pairs={{0,7},{1,6},{2,5},{3,4},{4,3},{5,2},{6,1},{7,0},{8,15},{9,14},{10,... | collective-permute-start | bytes 393224 | tf_op jit(solution)/shard_map/ppermute | solution.py:38
  300.8 25.4 %collective-permute-start.11 = (bf16[2,1,1,64,512]{4,3,0,2,1:T(8,128)(2,1)}, bf16[2,1,1,64,512]{4,3,0,2,1:T(8,128)(2,1)}, u32[]{:S(2)}, u32[]{:S(2)}) collective-permute-start(bf16[2,1,1,64,512]{4,3,0,2,1:T(8,128)(2,1)} %get-tuple-element.214), channel_id=1, source_target_pairs={{0,1},{1,0},{2,3},{3,2},{4,5},{5,4},{6,7},{7,6},{8,9},{9,8},{10,11... | collective-permute-start | bytes 393224 | tf_op jit(solution)/shard_map/ppermute | solution.py:38
  304.0 23.9 %collective-permute-start.12 = (bf16[2,1,1,64,512]{4,3,0,2,1:T(8,128)(2,1)}, bf16[2,1,1,64,512]{4,3,0,2,1:T(8,128)(2,1)}, u32[]{:S(2)}, u32[]{:S(2)}) collective-permute-start(bf16[2,1,1,64,512]{4,3,0,2,1:T(8,128)(2,1)} %get-tuple-element.213), channel_id=1, source_target_pairs={{0,2},{1,3},{2,0},{3,1},{4,6},{5,7},{6,4},{7,5},{8,10},{9,11},{10,... | collective-permute-start | bytes 393224 | tf_op jit(solution)/shard_map/ppermute | solution.py:38
  315.5 18.5 %collective-permute-start.13 = (bf16[2,1,1,64,512]{4,3,0,2,1:T(8,128)(2,1)}, bf16[2,1,1,64,512]{4,3,0,2,1:T(8,128)(2,1)}, u32[]{:S(2)}, u32[]{:S(2)}) collective-permute-start(bf16[2,1,1,64,512]{4,3,0,2,1:T(8,128)(2,1)} %get-tuple-element.212), channel_id=1, source_target_pairs={{0,3},{1,2},{2,1},{3,0},{4,7},{5,6},{6,5},{7,4},{8,11},{9,10},{10,... | collective-permute-start | bytes 393224 | tf_op jit(solution)/shard_map/ppermute | solution.py:38
  315.5 20.0 %collective-permute-start.14 = (bf16[2,1,1,64,512]{4,3,0,2,1:T(8,128)(2,1)}, bf16[2,1,1,64,512]{4,3,0,2,1:T(8,128)(2,1)}, u32[]{:S(2)}, u32[]{:S(2)}) collective-permute-start(bf16[2,1,1,64,512]{4,3,0,2,1:T(8,128)(2,1)} %get-tuple-element.211), channel_id=1, source_target_pairs={{0,4},{1,5},{2,6},{3,7},{4,0},{5,1},{6,2},{7,3},{8,12},{9,13},{10,... | collective-permute-start | bytes 393224 | tf_op jit(solution)/shard_map/ppermute | solution.py:38
  318.0 22.4 %collective-permute-start.15 = (bf16[2,1,1,64,512]{4,3,0,2,1:T(8,128)(2,1)}, bf16[2,1,1,64,512]{4,3,0,2,1:T(8,128)(2,1)}, u32[]{:S(2)}, u32[]{:S(2)}) collective-permute-start(bf16[2,1,1,64,512]{4,3,0,2,1:T(8,128)(2,1)} %get-tuple-element.210), channel_id=1, source_target_pairs={{0,5},{1,4},{2,7},{3,6},{4,1},{5,0},{6,3},{7,2},{8,13},{9,12},{10,... | collective-permute-start | bytes 393224 | tf_op jit(solution)/shard_map/ppermute | solution.py:38
  323.3 1.0 copy-start.7
  326.3 15.7 %collective-permute-start.16 = (bf16[2,1,1,64,512]{4,3,0,2,1:T(8,128)(2,1)}, bf16[2,1,1,64,512]{4,3,0,2,1:T(8,128)(2,1)S(1)}, u32[]{:S(2)}, u32[]{:S(2)}) collective-permute-start(bf16[2,1,1,64,512]{4,3,0,2,1:T(8,128)(2,1)} %get-tuple-element.209), channel_id=1, source_target_pairs={{0,6},{1,7},{2,4},{3,5},{4,2},{5,3},{6,0},{7,1},{8,14},{9,15},{10,... | collective-permute-start | bytes 393224 | tf_op jit(solution)/shard_map/ppermute | solution.py:38
  327.9 15.3 %collective-permute-start.17 = (bf16[2,1,1,64,512]{4,3,0,2,1:T(8,128)(2,1)}, bf16[2,1,1,64,512]{4,3,0,2,1:T(8,128)(2,1)S(1)}, u32[]{:S(2)}, u32[]{:S(2)}) collective-permute-start(bf16[2,1,1,64,512]{4,3,0,2,1:T(8,128)(2,1)} %get-tuple-element.208), channel_id=1, source_target_pairs={{0,7},{1,6},{2,5},{3,4},{4,3},{5,2},{6,1},{7,0},{8,15},{9,14},{10,... | collective-permute-start | bytes 393224 | tf_op jit(solution)/shard_map/ppermute | solution.py:38
  333.9 16.6 %collective-permute-start.4 = (bf16[2,1,1,64,512]{4,3,0,2,1:T(8,128)(2,1)}, bf16[2,1,1,64,512]{4,3,0,2,1:T(8,128)(2,1)}, u32[]{:S(2)}, u32[]{:S(2)}) collective-permute-start(bf16[2,1,1,64,512]{4,3,0,2,1:T(8,128)(2,1)} %get-tuple-element.221), channel_id=1, source_target_pairs={{0,1},{1,0},{2,3},{3,2},{4,5},{5,4},{6,7},{7,6},{8,9},{9,8},{10,11... | collective-permute-start | bytes 393224 | tf_op jit(solution)/shard_map/ppermute | solution.py:38
  335.5 16.8 %collective-permute-start.5 = (bf16[2,1,1,64,512]{4,3,0,2,1:T(8,128)(2,1)}, bf16[2,1,1,64,512]{4,3,0,2,1:T(8,128)(2,1)}, u32[]{:S(2)}, u32[]{:S(2)}) collective-permute-start(bf16[2,1,1,64,512]{4,3,0,2,1:T(8,128)(2,1)} %get-tuple-element.220), channel_id=1, source_target_pairs={{0,2},{1,3},{2,0},{3,1},{4,6},{5,7},{6,4},{7,5},{8,10},{9,11},{10,... | collective-permute-start | bytes 393224 | tf_op jit(solution)/shard_map/ppermute | solution.py:38
  340.4 17.5 %collective-permute-start.6 = (bf16[2,1,1,64,512]{4,3,0,2,1:T(8,128)(2,1)}, bf16[2,1,1,64,512]{4,3,0,2,1:T(8,128)(2,1)}, u32[]{:S(2)}, u32[]{:S(2)}) collective-permute-start(bf16[2,1,1,64,512]{4,3,0,2,1:T(8,128)(2,1)} %get-tuple-element.219), channel_id=1, source_target_pairs={{0,3},{1,2},{2,1},{3,0},{4,7},{5,6},{6,5},{7,4},{8,11},{9,10},{10,... | collective-permute-start | bytes 393224 | tf_op jit(solution)/shard_map/ppermute | solution.py:38
  342.0 17.5 %collective-permute-start.7 = (bf16[2,1,1,64,512]{4,3,0,2,1:T(8,128)(2,1)}, bf16[2,1,1,64,512]{4,3,0,2,1:T(8,128)(2,1)}, u32[]{:S(2)}, u32[]{:S(2)}) collective-permute-start(bf16[2,1,1,64,512]{4,3,0,2,1:T(8,128)(2,1)} %get-tuple-element.218), channel_id=1, source_target_pairs={{0,4},{1,5},{2,6},{3,7},{4,0},{5,1},{6,2},{7,3},{8,12},{9,13},{10,... | collective-permute-start | bytes 393224 | tf_op jit(solution)/shard_map/ppermute | solution.py:38
  343.3 18.3 %collective-permute-start.8 = (bf16[2,1,1,64,512]{4,3,0,2,1:T(8,128)(2,1)}, bf16[2,1,1,64,512]{4,3,0,2,1:T(8,128)(2,1)}, u32[]{:S(2)}, u32[]{:S(2)}) collective-permute-start(bf16[2,1,1,64,512]{4,3,0,2,1:T(8,128)(2,1)} %get-tuple-element.217), channel_id=1, source_target_pairs={{0,5},{1,4},{2,7},{3,6},{4,1},{5,0},{6,3},{7,2},{8,13},{9,12},{10,... | collective-permute-start | bytes 393224 | tf_op jit(solution)/shard_map/ppermute | solution.py:38
  350.6 12.5 %collective-permute-start.9 = (bf16[2,1,1,64,512]{4,3,0,2,1:T(8,128)(2,1)}, bf16[2,1,1,64,512]{4,3,0,2,1:T(8,128)(2,1)S(1)}, u32[]{:S(2)}, u32[]{:S(2)}) collective-permute-start(bf16[2,1,1,64,512]{4,3,0,2,1:T(8,128)(2,1)} %get-tuple-element.216), channel_id=1, source_target_pairs={{0,6},{1,7},{2,4},{3,5},{4,2},{5,3},{6,0},{7,1},{8,14},{9,15},{10,... | collective-permute-start | bytes 393224 | tf_op jit(solution)/shard_map/ppermute | solution.py:38
  352.3 26.2 %copy-start.13 = (pred[8]{0:T(512)(128)(4,1)S(1)}, pred[8]{0:T(512)(128)(4,1)}, u32[]{:S(2)}) copy-start(pred[8]{0:T(512)(128)(4,1)} %copy-done.12) | copy-start | bytes 28
  352.3 26.3 %copy-start.19 = (s32[8]{0:T(128)S(1)}, s32[8]{0:T(128)}, u32[]{:S(2)}) copy-start(s32[8]{0:T(128)} %copy-done.18) | copy-start | bytes 100
  352.3 11.5 %collective-permute-start.10 = (bf16[2,1,1,64,512]{4,3,0,2,1:T(8,128)(2,1)}, bf16[2,1,1,64,512]{4,3,0,2,1:T(8,128)(2,1)S(1)}, u32[]{:S(2)}, u32[]{:S(2)}) collective-permute-start(bf16[2,1,1,64,512]{4,3,0,2,1:T(8,128)(2,1)} %get-tuple-element.215), channel_id=1, source_target_pairs={{0,7},{1,6},{2,5},{3,4},{4,3},{5,2},{6,1},{7,0},{8,15},{9,14},{10,... | collective-permute-start | bytes 393224 | tf_op jit(solution)/shard_map/ppermute | solution.py:38
  367.4 13.2 %copy-start.15 = (pred[8]{0:T(512)(128)(4,1)S(1)}, pred[8]{0:T(512)(128)(4,1)}, u32[]{:S(2)}) copy-start(pred[8]{0:T(512)(128)(4,1)} %copy-done.14) | copy-start | bytes 28
  367.4 13.2 %copy-start.21 = (s32[8]{0:T(128)S(1)}, s32[8]{0:T(128)}, u32[]{:S(2)}) copy-start(s32[8]{0:T(128)} %copy-done.20) | copy-start | bytes 100
  375.8 5.7 %copy-start.17 = (pred[8]{0:T(512)(128)(4,1)S(1)}, pred[8]{0:T(512)(128)(4,1)}, u32[]{:S(2)}) copy-start(pred[8]{0:T(512)(128)(4,1)} %copy-done.16) | copy-start | bytes 28
  375.8 5.7 %copy-start.23 = (s32[8]{0:T(128)S(1)}, s32[8]{0:T(128)}, u32[]{:S(2)}) copy-start(s32[8]{0:T(128)} %copy-done.22) | copy-start | bytes 100
  375.8 4.8 %copy-start.1 = (bf16[8,2,64,512]{3,2,1,0:T(8,128)(2,1)S(1)}, bf16[8,2,64,512]{3,2,1,0:T(8,128)(2,1)}, u32[]{:S(2)}) copy-start(bf16[8,2,64,512]{3,2,1,0:T(8,128)(2,1)} %gather_fusion.4) | copy-start | bytes 3145732
  382.8 36.0 %collective-permute-start.25 = (bf16[256,5120]{1,0:T(8,128)(2,1)S(1)}, bf16[256,5120]{1,0:T(8,128)(2,1)S(1)}, u32[]{:S(2)}, u32[]{:S(2)}) collective-permute-start(bf16[256,5120]{1,0:T(8,128)(2,1)S(1)} %pad_maximum_fusion), channel_id=1, source_target_pairs={{8,0},{16,8},{24,16},{0,24},{9,1},{17,9},{25,17},{1,25},{10,2},{18... | collective-permute-start | bytes 7864328 | tf_op jit(solution)/shard_map/ppermute | solution.py:70
Sparse Core Ops, SparseCore 0:
  30.9 86.0 all-reduce.7
  279.7 95.4 all-reduce.5
